TPU v7x, 256 devices: a whole 4x4x8 slice. The times are simulated.
256 devices in a mesh: seq: 64 (over y, z, core), tr: 2 (over x_lo), tc: 2 (over x_hi).
Axes of the slice: x: 4 (x_hi: 2, x_lo: 2; x = x_hi * 2 + x_lo), y: 4, z: 8, core: 2. Of those that a mesh axis runs over, the one named last changes fastest.
Arguments:
- activations: bfloat16 [65536, 1024], P('seq', ('tr', 'tc')), may hold values from -6 to 6
- seg_len: int32 [64], P('seq'), may hold values from 1 to 1024, as said below
- seg_start: int32 [64], P('seq'), may hold values from 0 to 1, as said below
- memory_rates: float32 [3, 64, 8], P(None, 'seq'), may hold values from 0 to 1, as said below
- w_qkv: bfloat16 [1024, 3, 1024], P(None, None, ('tr', 'tc')), may hold values from -0.1875 to 0.1875
- conv_w: float32 [4, 3, 1024], P(None, None, ('tr', 'tc')), may hold values from -3 to 3
- persistent: bfloat16 [2, 16, 1024], P(None, None, ('tr', 'tc')), may hold values from -6 to 6
- w_out: bfloat16 [1024, 1024], P(('tr', 'tc')), may hold values from -0.1875 to 0.1875
- w_gate: bfloat16 [1024, 2816], P(None, ('tr', 'tc')), may hold values from -0.1875 to 0.1875
- w_up: bfloat16 [1024, 2816], P(None, ('tr', 'tc')), may hold values from -0.1875 to 0.1875
- w_down: bfloat16 [2816, 1024], P(('tr', 'tc')), may hold values from -0.109375 to 0.109375
Outputs:
- layer_out: bfloat16 [65536, 1024], P('seq', ('tr', 'tc'))
Inputs may be any that keep to these rules, and one draw needn't show every extreme that they name: `seg_start`: 1 where a segment begins a prompt, 0 where it continues the prompt of the segment before; segment 0 begins a prompt; a prompt spans at most 32 segments, and in every draw one prompt spans exactly that many. `seg_len`: live tokens at the head of each segment; every segment of a prompt but its last is full. `memory_rates`: all three tables lie strictly between 0 and 1.
All inputs are finite; a program needn't handle non-finite values.
Results may differ from a plain program's by a relative error of at most 0.015.
Values may be sent and summed in bfloat16 or wider, within the bound.
No kernel may reach another device: no remote copies, remote signals or barrier semaphores. Data moves between devices by JAX's collectives and lax.ppermute only.
A program may use at most 192 MiB of HBM per device.

v0:
```python
import jax
import jax.numpy as jnp
from jax import lax
from jax.sharding import PartitionSpec as P

HD = 128
SEG = 1024
CONV = 4
epsilon = 1e-06
score_scale = 8.0


def passed_along(block, axis, distance):
    devices = range(lax.axis_size(axis))
    route = [(i - distance, i) for i in devices if i - distance in devices]
    return lax.ppermute(block, axis, route)


def carried_in(array, axis, combine, identity):
    count, index = (lax.axis_size(axis), lax.axis_index(axis))
    everything = jax.tree.map(
        lambda part, kind: lax.all_gather(part.astype(kind), axis),
        array,
        (jnp.bfloat16, jnp.bfloat16),
    )
    start = jax.tree.map(
        lambda part, zero: jnp.broadcast_to(jnp.asarray(zero, part.dtype), part.shape),
        array,
        identity,
    )

    def step(k, before):
        reached = k < index
        new = combine(
            before, jax.tree.map(lambda part, own: part[k].astype(own.dtype), everything, array)
        )
        return jax.tree.map(lambda a, b: jnp.where(reached, a, b), new, before)

    return lax.fori_loop(0, count, step, start)


def unit_rows(values_in):
    return values_in * lax.rsqrt(jnp.sum(values_in * values_in, -1, keepdims=True) + epsilon)


def exact_product(left, right):
    return jnp.matmul(left, right, precision=lax.Precision.HIGHEST)


def combine(earlier, later):
    return (exact_product(later[0], earlier[0]), exact_product(later[0], earlier[1]) + later[1])


def body(
    activations,
    seg_len,
    seg_start,
    memory_rates,
    w_qkv,
    conv_w,
    persistent,
    w_out,
    w_gate,
    w_up,
    w_down,
):
    token_rows, local_feat = activations.shape
    seg_count = seg_len.shape[0]
    full_width = w_qkv.shape[0]
    head_width = w_qkv.shape[2]
    local_heads = head_width // HD
    group_index = lax.axis_index(("tr", "tc"))
    wide = w_qkv.reshape(full_width, 3 * head_width)
    row_ids = jnp.arange(token_rows, dtype=jnp.int32)
    position = row_ids % SEG
    segment_of = row_ids // SEG
    continuing = seg_start[segment_of] == 0
    piece = lax.all_gather(activations, ("tr", "tc"), axis=1, tiled=True)
    piece_f = piece.astype(jnp.float32)
    projected = jnp.dot(piece, wide, preferred_element_type=jnp.float32)
    squares = jnp.sum(piece_f * piece_f, -1)
    qkv = (projected * lax.rsqrt(squares / full_width + epsilon)[:, None]).astype(jnp.bfloat16)
    edge_rows = passed_along(qkv[token_rows - (CONV - 1) :], "seq", 1)
    extended = jnp.concatenate([edge_rows, qkv], 0)
    taps = conv_w.reshape(CONV, 3 * head_width)
    convolved = jnp.zeros((token_rows, 3 * head_width), jnp.float32)
    for offset in range(CONV):
        shifted = extended[CONV - 1 - offset : CONV - 1 - offset + token_rows].astype(jnp.float32)
        valid = (position >= offset) | continuing
        convolved = convolved + jnp.where(valid[:, None], taps[offset] * shifted, 0.0)
    parts = convolved.reshape(token_rows, 3, local_heads, HD)
    query_n = unit_rows(parts[:, 0]).astype(jnp.bfloat16)
    key_n = unit_rows(parts[:, 1]).astype(jnp.bfloat16)
    value_n = parts[:, 2].astype(jnp.bfloat16)
    pkeys = unit_rows(persistent[0].astype(jnp.float32).reshape(-1, local_heads, HD)).astype(
        jnp.bfloat16
    )
    pvalues = persistent[1].reshape(-1, local_heads, HD)
    persist_rows = pkeys.shape[0]
    live = position < seg_len[segment_of]
    keys_live = jnp.where(live[:, None, None], key_n, jnp.zeros((), jnp.bfloat16)).reshape(
        seg_count, SEG, local_heads, HD
    )
    value_segs = value_n.reshape(seg_count, SEG, local_heads, HD)
    a_mats = jnp.einsum("cthi,cthj->chij", keys_live, keys_live, preferred_element_type=jnp.float32)
    b_mats = jnp.einsum(
        "cthi,cthj->chij", keys_live, value_segs, preferred_element_type=jnp.float32
    )
    my_rates = lax.dynamic_slice_in_dim(memory_rates, group_index * local_heads, local_heads, 2)
    decay_factor = my_rates[0][:, :, None, None]
    eta = my_rates[1][:, :, None, None]
    theta = my_rates[2][:, :, None, None]
    keep = (1 - seg_start).astype(jnp.float32)[:, None, None, None]
    identity = jnp.eye(HD, dtype=jnp.float32)
    upper = jnp.concatenate([(1.0 - decay_factor) * identity - theta * a_mats, eta * identity], -1)
    lower = jnp.concatenate([-theta * a_mats, eta * identity], -1)
    seg_maps = jnp.concatenate([upper, lower], -2) * keep
    seg_shifts = jnp.concatenate([theta * b_mats, theta * b_mats], -2)
    dev_map = seg_maps[0]
    dev_shift = seg_shifts[0]
    neutral = (
        jnp.broadcast_to(jnp.eye(2 * HD, dtype=jnp.float32), dev_map.shape),
        jnp.zeros_like(dev_shift),
    )
    _, state = carried_in((dev_map, dev_shift), "seq", combine, neutral)
    seg_index = 0
    memory_in = state[:, :HD] * keep[seg_index]
    query_seg = query_n.astype(jnp.float32)
    retr_parts = jnp.einsum("thi,hij->thj", query_seg, memory_in, precision=lax.Precision.HIGHEST)
    mem = retr_parts * lax.rsqrt(jnp.mean(retr_parts * retr_parts, -1, keepdims=True) + epsilon)
    block_rows = min(512, SEG)
    attn_parts = []
    seg_index = 0
    first = seg_index * SEG
    keys_all = jnp.concatenate([pkeys, key_n], 0)
    values_all = jnp.concatenate([pvalues, value_n], 0)
    cols_k = jnp.arange(persist_rows + SEG, dtype=jnp.int32)[None, :] - persist_rows
    for block_start in range(0, SEG, block_rows):
        query_blk = query_n[first + block_start : first + block_start + block_rows]
        scores = score_scale * jnp.einsum(
            "qhd,khd->hqk", query_blk, keys_all, preferred_element_type=jnp.float32
        )
        rows_q = block_start + jnp.arange(block_rows, dtype=jnp.int32)[:, None]
        allow = (cols_k < 0) | (cols_k <= rows_q) & (cols_k < seg_len[seg_index])
        weights = jnp.where(allow[None], jnp.exp(scores), 0.0)
        probs = (weights / jnp.sum(weights, -1, keepdims=True)).astype(jnp.bfloat16)
        attn_parts.append(
            jnp.einsum("hqk,khd->qhd", probs, values_all, preferred_element_type=jnp.float32)
        )
    attn = jnp.concatenate(attn_parts, 0)
    heads_out = (attn + mem).astype(jnp.bfloat16).reshape(token_rows, head_width)
    partial_value = jnp.dot(heads_out, w_out, preferred_element_type=jnp.float32)
    share = lax.psum_scatter(
        partial_value.astype(jnp.bfloat16), ("tr", "tc"), scatter_dimension=1, tiled=True
    ).astype(jnp.float32)
    resid = (activations.astype(jnp.float32) + share).astype(jnp.bfloat16)
    piece = lax.all_gather(resid, ("tr", "tc"), axis=1, tiled=True)
    piece_f = piece.astype(jnp.float32)
    gate = jnp.dot(piece, w_gate, preferred_element_type=jnp.float32)
    up_proj = jnp.dot(piece, w_up, preferred_element_type=jnp.float32)
    squares2 = jnp.sum(piece_f * piece_f, -1)
    inv_rms2 = lax.rsqrt(squares2 / full_width + epsilon)[:, None]
    hidden = (jax.nn.silu(gate * inv_rms2) * (up_proj * inv_rms2)).astype(jnp.bfloat16)
    down = jnp.dot(hidden, w_down, preferred_element_type=jnp.float32)
    ffn_share = lax.psum_scatter(
        down.astype(jnp.bfloat16), ("tr", "tc"), scatter_dimension=1, tiled=True
    ).astype(jnp.float32)
    return (resid.astype(jnp.float32) + ffn_share).astype(jnp.bfloat16)


def solution(mesh):
    return jax.shard_map(
        body,
        mesh=mesh,
        in_specs=(
            P("seq", ("tr", "tc")),
            P("seq"),
            P("seq"),
            P(None, "seq", None),
            P(None, None, ("tr", "tc")),
            P(None, None, ("tr", "tc")),
            P(None, None, ("tr", "tc")),
            P(("tr", "tc"), None),
            P(None, ("tr", "tc")),
            P(None, ("tr", "tc")),
            P(("tr", "tc"), None),
        ),
        out_specs=P("seq", ("tr", "tc")),
        check_vma=False,
    )
```

profile of v0, /device:TPU:1, one launch (start us, length us, event | category | flops | bytes accessed | tf_op | source)
XLA Modules:
  0.0 545.9 jit_solution(447343479801649792)
XLA Ops:
  8.0 2.6 copy.46
  11.4 51.8 %all-gather.5.cloned.1.call-done = bf16[1024,1024]{1,0:T(8,128)(2,1)} async-done(((bf16[1024,256]{1,0:T(8,128)(2,1)}), bf16[1024,1024]{1,0:T(8,128)(2,1)}) %all-gather.5.cloned.1.call-update) | async-done | bytes 2097168 | tf_op jit(solution)/shard_map/all_gather | solution.py:78
  63.1 2.1 multiply_reduce_fusion.1
  65.2 3.9 multiply_convert_fusion
  69.1 3.6 collective-permute-start
  73.5 3.8 select_add_fusion
  77.3 5.2 reshape.355
  82.5 1.7 fusion.62
  84.2 1.6 slice.86
  91.1 2.2 fusion.15
  94.0 3.0 fusion.11
  97.0 5.4 fusion.20
  102.4 4.0 fusion.9
  106.4 5.3 fusion.21
  111.7 64.4 %all-gather.9.cloned.1.call-done = bf16[64,2,256,128]{3,2,1,0:T(8,128)(2,1)} async-done(((bf16[1,2,256,128]{3,2,1,0:T(8,128)(2,1)}), bf16[64,2,256,128]{3,2,1,0:T(8,128)(2,1)}) %all-gather.9.cloned.1.call-update) | async-done | bytes 8388624 | tf_op jit(solution)/shard_map/all_gather | solution.py:22
  176.1 98.8 %all-gather.7.cloned.1.call-done = bf16[64,2,256,256]{3,2,1,0:T(8,128)(2,1)} async-done(((bf16[1,2,256,256]{3,2,1,0:T(8,128)(2,1)}), bf16[64,2,256,256]{3,2,1,0:T(8,128)(2,1)}) %all-gather.7.cloned.1.call-update) | async-done | bytes 16777232 | tf_op jit(solution)/shard_map/all_gather | solution.py:22
  274.9 92.7 %while.14 = (s32[]{:T(128)}, f32[2,256,128]{2,1,0:T(8,128)S(1)}, s32[]{:T(128)}, bf16[64,2,256,256]{3,2,1,0:T(8,128)(2,1)}, bf16[64,2,256,128]{3,2,1,0:T(8,128)(2,1)}, /*index=5*/s32[]{:T(128)}, s32[]{:T(128)}) while((s32[]{:T(128)}, f32[2,256,128]{2,1,0:T(8,128)S(1)}, s32[]{:T(128)}, bf16[64,2,256,256]{3,2,1,0:T(8,128)(2,1)}, ...), condition=%wide.region_7.8_spmd.clone, body=%wide.region_6.7_spmd.clone.sunk | while | flops 201654272 | bytes 1706599 | solution.py:39
  275.0 1.4 fusion.83
  279.4 1.4 fusion.83
  280.8 1.4 fusion.83
  282.2 1.4 fusion.83
  283.7 1.4 fusion.83
  285.1 1.4 fusion.83
  369.7 3.2 convolution_convert_fusion
  373.0 45.7 %reduce-scatter.3.cloned.1.call-done = bf16[1024,256]{1,0:T(8,128)(2,1)} async-done(((bf16[1024,1024]{1,0:T(8,128)(2,1)}), bf16[1024,256]{1,0:T(8,128)(2,1)}) %reduce-scatter.3.cloned.1.call-update) | async-done | bytes 524304 | tf_op jit(solution)/shard_map/reduce_scatter | solution.py:153
  418.7 2.0 add_convert_fusion.1
  421.0 50.0 %all-gather.11.cloned.1.call-done = bf16[1024,1024]{1,0:T(8,128)(2,1)} async-done(((bf16[1024,256]{1,0:T(8,128)(2,1)}), bf16[1024,1024]{1,0:T(8,128)(2,1)}) %all-gather.11.cloned.1.call-update) | async-done | bytes 2097168 | tf_op jit(solution)/shard_map/all_gather | solution.py:157
  471.0 2.1 multiply_reduce_fusion
  473.1 4.9 fusion.64
  478.0 7.8 %convolution_convert_fusion.1 = bf16[1024,1024]{1,0:T(8,128)(2,1)} fusion(bf16[704,1024]{1,0:T(8,128)(2,1)S(1)} %copy-done, f32[1024,704]{0,1:T(8,128)} %fusion.64, bf16[1024,1024]{1,0:T(8,128)(2,1)} %all-gather.11.cloned.1.call-done, bf16[1024,704]{0,1:T(8,128)(2,1)} %param.22, f32[1024]{0:T(1024)S(1)} %add_rsqrt_fusion.3), kind=kOutput, calls=%fused_computation.31 | convolution fusion | flops 2959605760 | bytes 9965568 | tf_op jit(solution)/shard_map/dot_general | solution.py:164
  485.8 51.2 %reduce-scatter.5.cloned.1.call-done = bf16[1024,256]{1,0:T(8,128)(2,1)} async-done(((bf16[1024,1024]{1,0:T(8,128)(2,1)}), bf16[1024,256]{1,0:T(8,128)(2,1)}) %reduce-scatter.5.cloned.1.call-update) | async-done | bytes 524304 | tf_op jit(solution)/shard_map/reduce_scatter | solution.py:165
  537.1 2.0 add_convert_fusion
  (203 shorter events, 91.7 us)
Async XLA Ops:
  6.5 471.5 %copy-start = (bf16[704,1024]{1,0:T(8,128)(2,1)S(1)}, bf16[704,1024]{1,0:T(8,128)(2,1)}, u32[]{:S(2)}) copy-start(bf16[704,1024]{1,0:T(8,128)(2,1)} %param.23) | copy-start | bytes 4325380
  6.5 4.8 copy-start.9
  6.5 56.6 %all-gather.5.cloned.1.call-start = ((), (), s32[]{:S(2)}) async-start(), calls=%async_computation.2 | async-start | bytes 2621440 | tf_op jit(solution)/shard_map/all_gather | solution.py:78
  7.3 168.8 %all-gather.9.cloned.1.call-start = ((), (), s32[]{:S(2)}) async-start(), calls=%async_computation.4 | async-start | bytes 8519680 | tf_op jit(solution)/shard_map/all_gather | solution.py:22
  65.2 7.5 %copy-start.10 = (f32[3,1,8]{2,1,0:T(1,128)S(1)}, f32[3,1,8]{2,1,0:T(1,128)}, u32[]{:S(2)}) copy-start(f32[3,1,8]{2,1,0:T(1,128)} %param.16) | copy-start | bytes 292
  69.1 4.4 collective-permute-start
  86.5 3.1 copy-start.4
  86.5 4.3 copy-start.8
  86.6 0.9 copy-start.7
  88.8 186.2 %all-gather.7.cloned.1.call-start = ((), (), s32[]{:S(2)}) async-start(), calls=%async_computation.3 | async-start | bytes 17039360 | tf_op jit(solution)/shard_map/all_gather | solution.py:22
  90.5 328.2 %reduce-scatter.3.cloned.1.call-start = ((), (), s32[]{:S(2)}) async-start(), calls=%async_computation.5 | async-start | bytes 2621440 | tf_op jit(solution)/shard_map/reduce_scatter | solution.py:153
  91.0 3.0 copy-start.5
  97.0 5.4 copy-start.3
  274.9 93.5 %copy-start.6 = (f32[512,2,128]{0,2,1:T(8,128)S(1)}, f32[512,2,128]{0,2,1:T(8,128)}, u32[]{:S(2)}) copy-start(f32[512,2,128]{0,2,1:T(8,128)} %fusion.20) | copy-start | bytes 1572868
  369.7 49.0 %copy-start.2 = (bf16[1024,256]{1,0:T(8,128)(2,1)S(1)}, bf16[1024,256]{1,0:T(8,128)(2,1)}, u32[]{:S(2)}) copy-start(bf16[1024,256]{1,0:T(8,128)(2,1)} %param.13) | copy-start | bytes 1572868
  372.9 100.2 %copy-start.11 = (bf16[1024,704]{0,1:T(8,128)(2,1)S(1)}, bf16[1024,704]{0,1:T(8,128)(2,1)}, u32[]{:S(2)}) copy-start(bf16[1024,704]{0,1:T(8,128)(2,1)} %param.21) | copy-start | bytes 4325380
  372.9 98.1 %all-gather.11.cloned.1.call-start = ((), (), s32[]{:S(2)}) async-start(), calls=%async_computation.6 | async-start | bytes 2621440 | tf_op jit(solution)/shard_map/all_gather | solution.py:157
  420.7 116.4 %reduce-scatter.5.cloned.1.call-start = ((), (), s32[]{:S(2)}) async-start(), calls=%async_computation.7 | async-start | bytes 2621440 | tf_op jit(solution)/shard_map/reduce_scatter | solution.py:165
  478.0 59.1 %copy-start.1 = (bf16[1024,256]{1,0:T(8,128)(2,1)S(1)}, bf16[1024,256]{1,0:T(8,128)(2,1)}, u32[]{:S(2)}) copy-start(bf16[1024,256]{1,0:T(8,128)(2,1)} %add_convert_fusion.1) | copy-start | bytes 1572868
Sparse Core Ops, SparseCore 0:
  9.1 53.9 all-gather.4
  88.9 87.1 all-gather.8
  178.9 96.0 all-gather.6
  373.1 45.6 reduce-scatter.2
  420.8 50.1 all-gather.10
  486.0 51.0 reduce-scatter.4
where the time goes:
time: 548 us; the launch traced here: 546 us
  waiting for transfers between devices  363 us (66%)
  matrix products  128 us (23%)
  other arithmetic  17.2 us (3%)
  local copies, waits for them, and re-layouts  15.2 us (3%)
  between operations  15.1 us (3%)
    all_gather x2, waiting for transfers between devices, carried_in(): lax.all_gather(part.astype(kind), axis)  163 us
    dot_general x64, matrix products, exact_product(): return jnp.matmul(left, right, precision=lax.Precision.HIGHEST)  89 us
    all_gather x1, waiting for transfers between devices, body(): piece = lax.all_gather(activations, ('tr', 'tc'), axis=1, tiled=True)  51.8 us
    reduce_scatter x1, waiting for transfers between devices, body(): lax.psum_scatter(down.astype(jnp.bfloat16), ('tr', 'tc'), scatter_dimensi...  51.2 us
    all_gather x1, waiting for transfers between devices, body(): piece = lax.all_gather(resid, ('tr', 'tc'), axis=1, tiled=True)  50 us
    reduce_scatter x1, waiting for transfers between devices, body(): lax.psum_scatter(partial_value.astype(jnp.bfloat16), ('tr', 'tc'), scatte...  45.7 us
  transfers between devices with their start and end apart: 7, of which 7 were waited for; matrix products, arithmetic and copies ran while one was open for 5% of the time, Pallas kernels for 0%

commit v1 on v0

--- a/solution.py
+++ b/solution.py
@@ -154,7 +154,8 @@
         partial_value.astype(jnp.bfloat16), ("tr", "tc"), scatter_dimension=1, tiled=True
     ).astype(jnp.float32)
     resid = (activations.astype(jnp.float32) + share).astype(jnp.bfloat16)
-    piece = lax.all_gather(resid, ("tr", "tc"), axis=1, tiled=True)
+    sent = jnp.stack([resid] * lax.axis_size(("tr", "tc")))
+    piece = jnp.concatenate(lax.all_to_all(sent, ("tr", "tc"), 0, 0), axis=1)
     piece_f = piece.astype(jnp.float32)
     gate = jnp.dot(piece, w_gate, preferred_element_type=jnp.float32)
     up_proj = jnp.dot(piece, w_up, preferred_element_type=jnp.float32)

time: 548 us -> 520 us (0.949)
  waiting for transfers between devices: 363 us -> 312 us
  blocking collectives: 0 us -> 27.7 us
    all_gather x1 -> x0, waiting for transfers between devices: 50 us -> none  [body(): piece = lax.all_gather(resid, ('tr', 'tc'), axis=1, tiled=True)]
    all_to_all x0 -> x1, blocking collectives: none -> 27.7 us  [body(): piece = jnp.concatenate(lax.all_to_all(sent, ('tr', 'tc'), 0, 0), axis=1)]
  transfers between devices with their start and end apart: 7 -> 6, of which waited for: 7 -> 6; matrix products, arithmetic and copies ran while one was open for 5% -> 5% of each run, Pallas kernels for 0% -> 0%
where the time goes in v1:
time: 520 us; the launch traced here: 518 us
  waiting for transfers between devices  312 us (60%)
  matrix products  126 us (24%)
  blocking collectives  27.7 us (5%)
  local copies, waits for them, and re-layouts  16.3 us (3%)
  other arithmetic  15 us (3%)
  between operations  14.8 us (3%)
    all_gather x2, waiting for transfers between devices, carried_in(): lax.all_gather(part.astype(kind), axis)  163 us
    dot_general x64, matrix products, exact_product(): return jnp.matmul(left, right, precision=lax.Precision.HIGHEST)  89 us
    all_gather x1, waiting for transfers between devices, body(): piece = lax.all_gather(activations, ('tr', 'tc'), axis=1, tiled=True)  51.8 us
    reduce_scatter x1, waiting for transfers between devices, body(): lax.psum_scatter(down.astype(jnp.bfloat16), ('tr', 'tc'), scatter_dimensi...  50.2 us
    reduce_scatter x1, waiting for transfers between devices, body(): lax.psum_scatter(partial_value.astype(jnp.bfloat16), ('tr', 'tc'), scatte...  45.7 us
    all_to_all x1, blocking collectives, body(): piece = jnp.concatenate(lax.all_to_all(sent, ('tr', 'tc'), 0, 0), axis=1)  27.7 us
    dot_general x2, matrix products, body(): jnp.einsum('hqk,khd->qhd', probs, values_all, preferred_element_type=jnp....  10.7 us
  transfers between devices with their start and end apart: 6, of which 6 were waited for; matrix products, arithmetic and copies ran while one was open for 5% of the time, Pallas kernels for 0%

profile of v1, /device:TPU:1, one launch (start us, length us, event | category | flops | bytes accessed | tf_op | source)
XLA Modules:
  0.0 518.5 jit_solution(12935928732768936879)
XLA Ops:
  8.0 2.6 copy.48
  11.3 51.8 %all-gather.4.cloned.1.call-done = bf16[1024,1024]{1,0:T(8,128)(2,1)} async-done(((bf16[1024,256]{1,0:T(8,128)(2,1)}), bf16[1024,1024]{1,0:T(8,128)(2,1)}) %all-gather.4.cloned.1.call-update) | async-done | bytes 2097168 | tf_op jit(solution)/shard_map/all_gather | solution.py:78
  63.1 2.1 multiply_reduce_fusion.1
  65.2 3.9 multiply_convert_fusion
  69.1 3.6 collective-permute-start
  73.5 3.8 select_add_fusion
  77.3 5.2 %reshape.363 = f32[1024,3,2,128]{3,2,1,0:T(2,128)} reshape(f32[1024,768]{1,0:T(8,128)} %select_add_fusion) | data formatting | bytes 6291456 | tf_op jit(solution)/shard_map/reshape | solution.py:91
  82.5 1.7 fusion.62
  84.2 1.6 slice.86
  91.2 2.2 fusion.15
  94.1 3.0 fusion.11
  97.0 5.4 %fusion.20 = f32[512,2,128]{0,2,1:T(8,128)} fusion(f32[2,512,1040]{1,2,0:T(8,128)} %fusion.11, bf16[1024,2,128]{2,0,1:T(8,128)(2,1)} %bitcast.73, bf16[16,2,128]{2,0,1:T(8,128)(2,1)S(1)} %copy.50), kind=kOutput, calls=%fused_computation.38 | convolution fusion | flops 275826688 | bytes 5316608 | tf_op jit(solution)/shard_map/hqk,khd->qhd/dot_general | solution.py:148
  102.4 4.0 fusion.9
  106.4 5.3 %fusion.21 = f32[512,2,128]{0,2,1:T(8,128)} fusion(f32[2,512,1040]{1,2,0:T(8,128)} %fusion.9, bf16[1024,2,128]{2,0,1:T(8,128)(2,1)} %bitcast.74, bf16[16,2,128]{2,0,1:T(8,128)(2,1)S(1)} %copy.50), kind=kOutput, calls=%fused_computation.39 | convolution fusion | flops 275826688 | bytes 5316608 | tf_op jit(solution)/shard_map/hqk,khd->qhd/dot_general | solution.py:148
  111.7 64.4 %all-gather.8.cloned.1.call-done = bf16[64,2,256,128]{3,2,1,0:T(8,128)(2,1)} async-done(((bf16[1,2,256,128]{3,2,1,0:T(8,128)(2,1)}), bf16[64,2,256,128]{3,2,1,0:T(8,128)(2,1)}) %all-gather.8.cloned.1.call-update) | async-done | bytes 8388624 | tf_op jit(solution)/shard_map/all_gather | solution.py:22
  176.1 98.9 %all-gather.6.cloned.1.call-done = bf16[64,2,256,256]{3,2,1,0:T(8,128)(2,1)} async-done(((bf16[1,2,256,256]{3,2,1,0:T(8,128)(2,1)}), bf16[64,2,256,256]{3,2,1,0:T(8,128)(2,1)}) %all-gather.6.cloned.1.call-update) | async-done | bytes 16777232 | tf_op jit(solution)/shard_map/all_gather | solution.py:22
  275.0 92.7 %while.14 = (s32[]{:T(128)}, f32[2,256,128]{2,1,0:T(8,128)S(1)}, s32[]{:T(128)}, bf16[64,2,256,256]{3,2,1,0:T(8,128)(2,1)}, bf16[64,2,256,128]{3,2,1,0:T(8,128)(2,1)}, /*index=5*/s32[]{:T(128)}, s32[]{:T(128)}) while((s32[]{:T(128)}, f32[2,256,128]{2,1,0:T(8,128)S(1)}, s32[]{:T(128)}, bf16[64,2,256,256]{3,2,1,0:T(8,128)(2,1)}, ...), condition=%wide.region_7.8_spmd.clone, body=%wide.region_6.7_spmd.clone.sunk | while | flops 201654272 | bytes 1706599 | solution.py:39
  275.0 1.4 fusion.83
  276.5 1.4 fusion.83
  278.0 1.4 fusion.83
  279.4 1.4 fusion.83
  280.9 1.4 fusion.83
  282.3 1.4 fusion.83
  283.8 1.4 fusion.83
  285.2 1.4 fusion.83
  369.8 3.2 convolution_convert_fusion
  373.1 45.7 %reduce-scatter.3.cloned.1.call-done = bf16[1024,256]{1,0:T(8,128)(2,1)} async-done(((bf16[1024,1024]{1,0:T(8,128)(2,1)}), bf16[1024,256]{1,0:T(8,128)(2,1)}) %reduce-scatter.3.cloned.1.call-update) | async-done | bytes 524304 | tf_op jit(solution)/shard_map/reduce_scatter | solution.py:153
  421.1 27.7 %all_to_all.5 = bf16[4,1024,256]{1,2,0:T(8,128)(2,1)S(1)} all-to-all(bf16[4,1024,256]{1,2,0:T(8,128)(2,1)S(1)} %stack.2), channel_id=1, replica_groups=mesh['seq'=64,'tr'=2,'tc'=2] {'tr','tc'}, dimensions={0} | all-to-all | bytes 4194304 | tf_op jit(solution)/shard_map/all_to_all | solution.py:158
  449.3 3.2 fusion.64
  452.5 7.1 %convolution_convert_fusion.1 = bf16[1024,1024]{1,0:T(8,128)(2,1)} fusion(bf16[704,1024]{1,0:T(8,128)(2,1)S(1)} %copy-done, f32[1024,704]{0,1:T(8,128)} %fusion.64, bf16[1024,704]{0,1:T(8,128)(2,1)} %param.22, bf16[1024,1024]{0,1:T(8,128)(2,1)S(1)} %bitcast.69, f32[1024]{0:T(1024)S(1)} %add_rsqrt_fusion.3), kind=kOutput, calls=%fused_computation.31 | convolution fusion | flops 2959605760 | bytes 9965568 | tf_op jit(solution)/shard_map/dot_general | solution.py:165
  459.7 50.2 %reduce-scatter.5.cloned.1.call-done = bf16[1024,256]{1,0:T(8,128)(2,1)} async-done(((bf16[1024,1024]{1,0:T(8,128)(2,1)}), bf16[1024,256]{1,0:T(8,128)(2,1)}) %reduce-scatter.5.cloned.1.call-update) | async-done | bytes 524304 | tf_op jit(solution)/shard_map/reduce_scatter | solution.py:166
  509.8 2.1 add_convert_fusion
  (203 shorter events, 91.4 us)
Async XLA Ops:
  6.5 446.0 %copy-start = (bf16[704,1024]{1,0:T(8,128)(2,1)S(1)}, bf16[704,1024]{1,0:T(8,128)(2,1)}, u32[]{:S(2)}) copy-start(bf16[704,1024]{1,0:T(8,128)(2,1)} %param.23) | copy-start | bytes 4325380
  6.5 4.7 copy-start.9
  6.5 56.6 %all-gather.4.cloned.1.call-start = ((), (), s32[]{:S(2)}) async-start(), calls=%async_computation.3 | async-start | bytes 2621440 | tf_op jit(solution)/shard_map/all_gather | solution.py:78
  7.3 168.9 %all-gather.8.cloned.1.call-start = ((), (), s32[]{:S(2)}) async-start(), calls=%async_computation.5 | async-start | bytes 8519680 | tf_op jit(solution)/shard_map/all_gather | solution.py:22
  65.2 7.6 %copy-start.10 = (f32[3,1,8]{2,1,0:T(1,128)S(1)}, f32[3,1,8]{2,1,0:T(1,128)}, u32[]{:S(2)}) copy-start(f32[3,1,8]{2,1,0:T(1,128)} %param.16) | copy-start | bytes 292
  69.1 4.4 collective-permute-start
  86.5 3.2 copy-start.4
  86.5 4.3 copy-start.8
  86.6 0.9 copy-start.7
  88.8 186.2 %all-gather.6.cloned.1.call-start = ((), (), s32[]{:S(2)}) async-start(), calls=%async_computation.4 | async-start | bytes 17039360 | tf_op jit(solution)/shard_map/all_gather | solution.py:22
  90.6 328.2 %reduce-scatter.3.cloned.1.call-start = ((), (), s32[]{:S(2)}) async-start(), calls=%async_computation.6 | async-start | bytes 2621440 | tf_op jit(solution)/shard_map/reduce_scatter | solution.py:153
  91.1 3.0 copy-start.5
  97.0 5.4 %copy-start.3 = (pred[512,1040]{0,1:T(8,128)(4,1)S(1)}, pred[512,1040]{0,1:T(8,128)(4,1)}, u32[]{:S(2)}) copy-start(pred[512,1040]{0,1:T(8,128)(4,1)} %get-tuple-element.150) | copy-start | bytes 1597444
  275.0 93.5 %copy-start.6 = (f32[512,2,128]{0,2,1:T(8,128)S(1)}, f32[512,2,128]{0,2,1:T(8,128)}, u32[]{:S(2)}) copy-start(f32[512,2,128]{0,2,1:T(8,128)} %fusion.20) | copy-start | bytes 1572868
  369.8 49.0 %copy-start.2 = (bf16[1024,256]{1,0:T(8,128)(2,1)S(1)}, bf16[1024,256]{1,0:T(8,128)(2,1)}, u32[]{:S(2)}) copy-start(bf16[1024,256]{1,0:T(8,128)(2,1)} %param.13) | copy-start | bytes 1572868
  373.0 136.8 %reduce-scatter.5.cloned.1.call-start = ((), (), s32[]{:S(2)}) async-start(), calls=%async_computation.7 | async-start | bytes 2621440 | tf_op jit(solution)/shard_map/reduce_scatter | solution.py:166
  420.0 0.8 copy-start.1
  421.1 28.2 %copy-start.11 = (bf16[1024,704]{0,1:T(8,128)(2,1)S(1)}, bf16[1024,704]{0,1:T(8,128)(2,1)}, u32[]{:S(2)}) copy-start(bf16[1024,704]{0,1:T(8,128)(2,1)} %param.21) | copy-start | bytes 4325380
Sparse Core Ops, SparseCore 0:
  9.1 53.9 all-gather.3
  88.9 87.1 all-gather.7
  178.9 96.0 all-gather.5
  373.1 45.6 reduce-scatter.2
  459.8 50.0 reduce-scatter.4
